TPU v7x, 32 devices: a whole 2x2x4 slice. The times are simulated.
32 devices in a mesh: region: 4 (over y, x), col: 8 (over z, core).
Axes of the slice: x: 2, y: 2, z: 4, core: 2. Of those that a mesh axis runs over, the one named last changes fastest.
Arguments:
- tiles: float32 [1536, 128, 128], P(('region', 'col')), may hold values from -0.109375 to 0.109375
- tile_rows: int32 [1536], P(('region', 'col')), may hold values from 0 to 1
- tile_cols: int32 [1536], P(('region', 'col')), may hold values from 0 to 15
- tile_count: int32 [32], P(('region', 'col')), may hold values from 12 to 48, as said below
- rhs: float32 [64, 128], P(('region', 'col')), may hold values from -6 to 6
- base_cost: float32 [64, 128], P(('region', 'col')), may hold values from 0.1 to 1
- upper: float32 [64, 128], P(('region', 'col')), may hold values from 0.5 to 4
- primal: float32 [64, 16, 128], P(('region', 'col')), may hold values from 0 to 1
- dual: float32 [64, 16, 128], P(('region', 'col')), may hold values from 0 to 1
- price_levels: float32 [32, 128], replicated, may hold values from 0.5 to 2
- scenario_ids: int32 [16], replicated, may hold values from 0 to 31
Outputs:
- primal_out: float32 [64, 16, 128], P(('region', 'col'))
- dual_out: float32 [64, 16, 128], P(('region', 'col'))
- weight_out: float32 [16], replicated
Inputs may be any that keep to these rules, and one draw needn't show every extreme that they name: `tile_count`: slots at or past a device's count are padding and hold no part of the matrix; in every draw some device has all 48 slots live.
All inputs are finite; a program needn't handle non-finite values.
Results may differ from a plain program's by a relative error of at most 0.0001.
Values sent between devices are 32-bit elements; how exact they have to be, the bound alone decides.
No kernel may reach another device: no remote copies, remote signals or barrier semaphores. Data moves between devices by JAX's collectives and lax.ppermute only.
A program may use at most 64 MiB of HBM per device.

v0:
```python
import jax
import jax.numpy as jnp
from jax import lax
from jax.sharding import PartitionSpec as P

ITERS = 2


def local(
    tiles,
    tile_rows,
    tile_cols,
    tile_count,
    rhs,
    base_cost,
    upper,
    primal,
    dual,
    price_levels,
    scenario_ids,
):
    hp = lax.Precision.HIGHEST
    ntiles = tiles.shape[0]
    row_blocks = rhs.shape[0]
    own_blocks = base_cost.shape[0]
    scenarios = primal.shape[1]
    lanes = primal.shape[2]
    region_blocks = own_blocks * lax.axis_size("col")
    devices = lax.axis_size(("region", "col"))
    live = (jnp.arange(ntiles, dtype=jnp.int32) < tile_count[0]).astype(jnp.float32)
    row_select = (tile_rows[:, None] == jnp.arange(row_blocks, dtype=jnp.int32)[None, :]).astype(
        jnp.float32
    )
    row_live = row_select * live[:, None]
    col_select = (tile_cols[:, None] == jnp.arange(region_blocks, dtype=jnp.int32)[None, :]).astype(
        jnp.float32
    )
    col_live = col_select * live[:, None]
    choose = (
        scenario_ids[:, None] == jnp.arange(price_levels.shape[0], dtype=jnp.int32)[None, :]
    ).astype(jnp.float32)
    factor = jnp.dot(choose, price_levels, precision=hp)
    cost = base_cost[:, None, :] * factor[None, :, :]
    local_a = jnp.sum(jnp.sum(tiles * tiles, axis=(1, 2)) * live)
    local_c = jnp.sum(cost * cost, axis=(0, 2))
    local_b = jnp.sum(rhs * rhs)
    sq_a, sq_c, sq_b = lax.psum((local_a, local_c, local_b), ("region", "col"))
    eta = 0.5 / jnp.sqrt(sq_a / (lanes * row_blocks * devices))
    weight = jnp.sqrt(sq_c) / jnp.sqrt(sq_b)
    width = scenarios * lanes
    for step in range(ITERS):
        tau = (eta / weight)[None, :, None]
        sigma = (eta * weight)[None, :, None]
        dual_rows = jnp.dot(row_select, dual.reshape(row_blocks, width), precision=hp).reshape(
            ntiles, scenarios, lanes
        )
        contrib = jnp.einsum("tij,tsi->tsj", tiles, dual_rows, precision=hp)
        flat_terms = contrib.reshape(ntiles, width)
        partial_value = jnp.dot(col_live.T, flat_terms, precision=hp).reshape(
            region_blocks, scenarios, lanes
        )
        grad = lax.psum_scatter(partial_value, "col", scatter_dimension=0, tiled=True)
        new_primal = jnp.clip(primal - tau * (cost - grad), 0.0, upper[:, None, :])
        point = 2.0 * new_primal - primal
        region_point = lax.all_gather(point, "col", axis=0, tiled=True)
        selected = jnp.dot(
            col_select, region_point.reshape(region_blocks, width), precision=hp
        ).reshape(ntiles, scenarios, lanes)
        image = jnp.einsum("tij,tsj->tsi", tiles, selected, precision=hp)
        product = jnp.dot(row_live.T, image.reshape(ntiles, width), precision=hp).reshape(
            row_blocks, scenarios, lanes
        )
        new_dual = jnp.maximum(dual + sigma * (rhs[:, None, :] - product), 0.0)
        local_x = jnp.sum((new_primal - primal) ** 2, axis=(0, 2))
        local_y = jnp.sum((new_dual - dual) ** 2, axis=(0, 2))
        step_x = lax.psum(local_x, ("region", "col"))
        step_y = lax.psum(local_y, ("region", "col"))
        weight = jnp.sqrt(weight * jnp.sqrt((step_x + 1e-06) / (step_y + 1e-06)))
        primal, dual = (new_primal, new_dual)
    return (primal, dual, weight)


def solution(mesh):
    placed = (
        P(("region", "col"), None, None),
        P(("region", "col")),
        P(("region", "col")),
        P(("region", "col")),
        P(("region", "col"), None),
        P(("region", "col"), None),
        P(("region", "col"), None),
        P(("region", "col"), None, None),
        P(("region", "col"), None, None),
        P(),
        P(),
    )
    return jax.shard_map(
        local,
        mesh=mesh,
        in_specs=placed,
        out_specs=(P(("region", "col"), None, None), P(("region", "col"), None, None), P()),
        check_vma=False,
    )
```

profile of v0, /device:TPU:10, one launch (start us, length us, event | category | flops | bytes accessed | tf_op | source)
XLA Modules:
  0.0 194.1 jit_solution(15329960555821616585)
XLA Ops:
  7.2 0.0 copy-start
  7.2 0.0 copy-start.1
  7.2 0.0 copy-start.7
  7.2 0.0 reduce-scatter.3.cloned.1.call-start
  8.1 1.2 fusion.37
  9.3 0.0 copy-start.10
  9.3 0.0 copy-start.5
  9.3 0.0 copy-start.9
  9.3 0.0 copy-start.3
  9.3 0.0 copy-start.8
  9.3 4.7 %fusion.18 = f32[48,16,128]{2,1,0:T(8,128)S(1)} fusion(f32[48,128,128]{2,1,0:T(8,128)} %param.11, f32[48,16,128]{2,0,1:T(8,128)S(1)} %fusion.37), kind=kOutput, calls=%fused_computation.23 | convolution fusion | flops 150994944 | bytes 3932160 | tf_op jit(solution)/shard_map/tij,tsi->tsj/dot_general | solution.py:57
  14.1 0.0 copy-done.7
  14.1 0.4 fusion.9
  14.5 0.7 copy.80
  15.2 0.0 reduce-scatter.3.cloned.1.call-update
  15.2 0.0 reduce-scatter.5.cloned.1.call-start
  15.2 0.0 copy-done.1
  15.3 0.5 multiply_reduce_fusion
  15.7 0.0 copy-start.6
  15.7 0.0 copy-start.2
  15.7 0.6 fusion.68
  16.3 0.0 copy-done
  16.3 0.0 copy-done.10
  16.3 0.2 fusion.52
  16.5 0.0 copy-done.5
  16.5 0.1 fusion.26
  16.6 0.0 copy-done.9
  16.6 0.6 multiply_reduce_fusion.5
  17.2 41.5 %all-reduce.2 = (f32[16]{0:T(128)S(1)}, f32[]{:T(128)}, f32[]{:T(128)}) all-reduce(f32[16]{0:T(128)S(1)} %fusion.26, f32[]{:T(128)} %fusion.68, f32[]{:T(128)} %multiply_reduce_fusion.5), channel_id=1, replica_groups=mesh['region'=4,'col'=8] {'region','col'}, use_global_device_ids=true, to_apply=%region_6.0 | all-reduce | flops 18 | bytes 144 | tf_op jit(solution)/shard_map/psum | solution.py:47
  60.2 0.0 reduce-scatter.3.cloned.1.call-done
  60.2 0.0 copy-done.3
  60.2 0.0 copy-done.8
  60.2 0.9 multiply_reduce_fusion.4
  61.1 13.1 %all_gather.6 = f32[16,16,128]{2,1,0:T(8,128)S(1)} all-gather(f32[2,16,128]{2,1,0:T(8,128)S(1)} %multiply_subtract_fusion.3), channel_id=1, replica_groups=mesh['region'=4,'col'=8] {'col'}, dimensions={0}, use_global_device_ids=true | all-gather | bytes 147456 | tf_op jit(solution)/shard_map/all_gather | solution.py:65
  74.2 0.4 fusion.23
  74.6 5.0 %fusion.16 = f32[48,16,128]{2,1,0:T(8,128)S(1)} fusion(f32[48,128,128]{2,1,0:T(8,128)S(1)} %copy-done.1, f32[48,16,128]{2,0,1:T(8,128)S(1)} %fusion.23), kind=kOutput, calls=%fused_computation.21 | convolution fusion | flops 150994944 | bytes 3932160 | tf_op jit(solution)/shard_map/tij,tsj->tsi/dot_general | solution.py:69
  79.5 0.0 copy-done.6
  79.5 0.4 fusion.6
  80.0 0.0 copy-done.2
  80.0 0.2 multiply_reduce_fusion.3
  80.2 0.4 fusion.35
  80.6 2.9 %fusion.14 = f32[48,16,128]{2,1,0:T(8,128)S(1)} fusion(f32[48,128,128]{2,1,0:T(8,128)S(1)} %copy-done.1, f32[48,16,128]{2,0,1:T(8,128)S(1)} %fusion.35), kind=kOutput, calls=%fused_computation.19 | convolution fusion | flops 150994944 | bytes 3932160 | tf_op jit(solution)/shard_map/tij,tsi->tsj/dot_general | solution.py:57
  83.4 0.4 fusion.3
  83.9 0.7 copy.87
  84.5 0.0 reduce-scatter.5.cloned.1.call-update
  84.6 40.5 %all-reduce.1 = (f32[16]{0:T(128)S(1)}, f32[16]{0:T(128)S(1)}) all-reduce(f32[16]{0:T(128)S(1)} %get-tuple-element.30, f32[16]{0:T(128)S(1)} %get-tuple-element.28), channel_id=1, replica_groups=mesh['region'=4,'col'=8] {'region','col'}, use_global_device_ids=true, to_apply=%region_11.12 | all-reduce | flops 32 | bytes 256 | tf_op jit(solution)/shard_map/psum | solution.py:77
  125.1 0.0 reduce-scatter.5.cloned.1.call-done
  125.1 0.9 multiply_reduce_fusion.2
  126.0 0.0 copy-start.4
  126.0 12.4 %all_gather.7 = f32[16,16,128]{2,1,0:T(8,128)S(1)} all-gather(f32[2,16,128]{2,1,0:T(8,128)S(1)} %multiply_subtract_fusion.2), channel_id=1, replica_groups=mesh['region'=4,'col'=8] {'col'}, dimensions={0}, use_global_device_ids=true | all-gather | bytes 147456 | tf_op jit(solution)/shard_map/all_gather | solution.py:65
  138.4 0.4 fusion.20
  138.8 5.0 %fusion.12 = f32[48,16,128]{2,1,0:T(8,128)S(1)} fusion(f32[48,128,128]{2,1,0:T(8,128)S(1)} %copy-done.1, f32[48,16,128]{2,0,1:T(8,128)S(1)} %fusion.20), kind=kOutput, calls=%fused_computation.17 | convolution fusion | flops 150994944 | bytes 3932160 | tf_op jit(solution)/shard_map/tij,tsj->tsi/dot_general | solution.py:69
  143.8 0.4 fusion
  144.2 0.8 multiply_reduce_fusion.1
  145.0 41.7 %all-reduce = (f32[16]{0:T(128)S(1)}, f32[16]{0:T(128)S(1)}) all-reduce(f32[16]{0:T(128)S(1)} %get-tuple-element.24, f32[16]{0:T(128)S(1)} %get-tuple-element.22), channel_id=1, replica_groups=mesh['region'=4,'col'=8] {'region','col'}, use_global_device_ids=true, to_apply=%region_16.17 | all-reduce | flops 32 | bytes 256 | tf_op jit(solution)/shard_map/psum | solution.py:77
  186.7 0.5 multiply_sqrt_fusion
  187.2 0.0 copy-done.4
  (6 shorter events, 0.0 us)
Async XLA Ops:
  7.2 9.2 %copy-start = (f32[32,128]{1,0:T(8,128)S(1)}, f32[32,128]{1,0:T(8,128)}, u32[]{:S(2)}) copy-start(f32[32,128]{1,0:T(8,128)} %param.20) | copy-start | bytes 49156
  7.2 8.1 %copy-start.1 = (f32[48,128,128]{2,1,0:T(8,128)S(1)}, f32[48,128,128]{2,1,0:T(8,128)}, u32[]{:S(2)}) copy-start(f32[48,128,128]{2,1,0:T(8,128)} %param.11) | copy-start | bytes 9437188
  7.2 6.9 %copy-start.7 = (s32[48]{0:T(128)S(1)}, s32[48]{0:T(128)}, u32[]{:S(2)}) copy-start(s32[48]{0:T(128)} %param.13) | copy-start | bytes 580
  7.2 53.0 %reduce-scatter.3.cloned.1.call-start = ((), (), s32[]{:S(2)}) async-start(), calls=%async_computation.2 | async-start | bytes 147456 | tf_op jit(solution)/shard_map/reduce_scatter | solution.py:62
  9.3 7.0 %copy-start.10 = (s32[16]{0:T(128)S(1)}, s32[16]{0:T(128)}, u32[]{:S(2)}) copy-start(s32[16]{0:T(128)} %param.21) | copy-start | bytes 196
  9.3 7.2 %copy-start.5 = (f32[2,128]{1,0:T(2,128)S(1)}, f32[2,128]{1,0:T(2,128)}, u32[]{:S(2)}) copy-start(f32[2,128]{1,0:T(2,128)} %param.16) | copy-start | bytes 3076
  9.3 7.3 %copy-start.9 = (f32[2,128]{1,0:T(2,128)S(1)}, f32[2,128]{1,0:T(2,128)}, u32[]{:S(2)}) copy-start(f32[2,128]{1,0:T(2,128)} %param.15) | copy-start | bytes 3076
  9.3 50.9 %copy-start.3 = (f32[2,16,128]{2,1,0:T(8,128)S(1)}, f32[2,16,128]{2,1,0:T(8,128)}, u32[]{:S(2)}) copy-start(f32[2,16,128]{2,1,0:T(8,128)} %param.18) | copy-start | bytes 49156
  9.3 50.9 %copy-start.8 = (f32[2,128]{1,0:T(2,128)S(1)}, f32[2,128]{1,0:T(2,128)}, u32[]{:S(2)}) copy-start(f32[2,128]{1,0:T(2,128)} %param.17) | copy-start | bytes 3076
  15.2 109.9 %reduce-scatter.5.cloned.1.call-start = ((), (), s32[]{:S(2)}) async-start(), calls=%async_computation.3 | async-start | bytes 147456 | tf_op jit(solution)/shard_map/reduce_scatter | solution.py:62
  15.7 63.8 %copy-start.6 = (s32[48]{0:T(128)S(1)}, s32[48]{0:T(128)}, u32[]{:S(2)}) copy-start(s32[48]{0:T(128)} %param.12) | copy-start | bytes 580
  15.7 64.3 %copy-start.2 = (f32[2,16,128]{2,1,0:T(8,128)S(1)}, f32[2,16,128]{2,1,0:T(8,128)}, u32[]{:S(2)}) copy-start(f32[2,16,128]{2,1,0:T(8,128)} %param.19) | copy-start | bytes 49156
  126.0 61.2 %copy-start.4 = (f32[2,16,128]{2,1,0:T(8,128)}, f32[2,16,128]{2,1,0:T(8,128)S(1)}, u32[]{:S(2)}) copy-start(f32[2,16,128]{2,1,0:T(8,128)S(1)} %get-tuple-element.23) | copy-start | bytes 49156
Sparse Core Ops, SparseCore 0:
  15.3 27.7 reduce-scatter.2
  84.7 26.8 reduce-scatter.4
where the time goes:
time: 195 us; the launch traced here: 194 us
  blocking collectives  149 us (76%)
  matrix products  21.7 us (11%)
  between operations  16.4 us (8%)
  other arithmetic  5.15 us (3%)
    psum x2, blocking collectives, local(): step_y = lax.psum(local_y, ('region', 'col'))  82.2 us
    psum x1, blocking collectives, local(): sq_a, sq_c, sq_b = lax.psum((local_a, local_c, local_b), ('region', 'col'))  41.5 us
    all_gather x2, blocking collectives, local(): region_point = lax.all_gather(point, 'col', axis=0, tiled=True)  25.5 us
    dot_general x2, matrix products, local(): image = jnp.einsum('tij,tsj->tsi', tiles, selected, precision=hp)  9.98 us
    dot_general x2, matrix products, local(): contrib = jnp.einsum('tij,tsi->tsj', tiles, dual_rows, precision=hp)  7.59 us
  transfers between devices with their start and end apart: 2, of which 0 were waited for; matrix products, arithmetic and copies ran while one was open for 1% of the time, Pallas kernels for 0%

commit v1 on v0

--- a/solution.py
+++ b/solution.py
@@ -74,7 +74,13 @@
         local_x = jnp.sum((new_primal - primal) ** 2, axis=(0, 2))
         local_y = jnp.sum((new_dual - dual) ** 2, axis=(0, 2))
         step_x = lax.psum(local_x, ("region", "col"))
-        step_y = lax.psum(local_y, ("region", "col"))
+
+        def _pass_seats_all(q_in):
+            opened = lax.psum(q_in, axis_name="col")
+            long_array = lax.psum(opened, axis_name="region")
+            return long_array
+
+        step_y = _pass_seats_all(local_y)
         weight = jnp.sqrt(weight * jnp.sqrt((step_x + 1e-06) / (step_y + 1e-06)))
         primal, dual = (new_primal, new_dual)
     return (primal, dual, weight)

time: 195 us -> 271 us (1.39)
  blocking collectives: 149 us -> 198 us
  waiting for transfers between devices: 0.07 us -> 25.9 us
    psum x2 -> x6, blocking collectives: 82.2 us -> 129 us  [the longest x2 86.2 us: local(): step_x = lax.psum(local_x, ('region', 'col'))]
    reduce_scatter x2, waiting for transfers between devices: 0.04 us -> 25.9 us  [local(): lax.psum_scatter(partial_value, 'col', scatter_dimension=0, tiled=True)]
  transfers between devices with their start and end apart: 2 -> 2, of which waited for: 0 -> 1; matrix products, arithmetic and copies ran while one was open for 1% -> 1% of each run, Pallas kernels for 0% -> 0%
where the time goes in v1:
time: 271 us; the launch traced here: 269 us
  blocking collectives  198 us (73%)
  waiting for transfers between devices  25.9 us (10%)
  matrix products  21.7 us (8%)
  between operations  16.4 us (6%)
  other arithmetic  5.15 us (2%)
    psum x2, blocking collectives, local(): step_x = lax.psum(local_x, ('region', 'col'))  86.2 us
    psum x1, blocking collectives, local(): sq_a, sq_c, sq_b = lax.psum((local_a, local_c, local_b), ('region', 'col'))  41.5 us
    all_gather x2, blocking collectives, local(): region_point = lax.all_gather(point, 'col', axis=0, tiled=True)  27.2 us
    psum x2, blocking collectives, _pass_seats_all(): opened = lax.psum(q_in, axis_name='col')  27 us
    reduce_scatter x2, waiting for transfers between devices, local(): lax.psum_scatter(partial_value, 'col', scatter_dimension=0, tiled=True)  25.9 us
    psum x2, blocking collectives, _pass_seats_all(): long_array = lax.psum(opened, axis_name='region')  16.2 us
    dot_general x2, matrix products, local(): image = jnp.einsum('tij,tsj->tsi', tiles, selected, precision=hp)  9.98 us
    dot_general x2, matrix products, local(): contrib = jnp.einsum('tij,tsi->tsj', tiles, dual_rows, precision=hp)  7.59 us
  transfers between devices with their start and end apart: 2, of which 1 were waited for; matrix products, arithmetic and copies ran while one was open for 1% of the time, Pallas kernels for 0%

profile of v1, /device:TPU:10, one launch (start us, length us, event | category | flops | bytes accessed | tf_op | source)
XLA Modules:
  0.0 268.8 jit_solution(5853221392312416262)
XLA Ops:
  7.2 0.0 copy-start
  7.2 0.0 copy-start.1
  7.2 0.0 copy-start.7
  7.2 0.0 reduce-scatter.3.cloned.1.call-start
  8.1 1.2 fusion.37
  9.3 0.0 copy-start.10
  9.3 0.0 copy-start.5
  9.3 0.0 copy-start.9
  9.3 0.0 copy-start.3
  9.3 0.0 copy-start.8
  9.3 4.7 %fusion.18 = f32[48,16,128]{2,1,0:T(8,128)S(1)} fusion(f32[48,128,128]{2,1,0:T(8,128)} %param.11, f32[48,16,128]{2,0,1:T(8,128)S(1)} %fusion.37), kind=kOutput, calls=%fused_computation.23 | convolution fusion | flops 150994944 | bytes 3932160 | tf_op jit(solution)/shard_map/tij,tsi->tsj/dot_general | solution.py:57
  14.1 0.0 copy-done.7
  14.1 0.4 fusion.9
  14.5 0.7 copy.80
  15.2 0.0 reduce-scatter.3.cloned.1.call-update
  15.2 0.0 reduce-scatter.5.cloned.1.call-start
  15.2 0.0 copy-done.1
  15.3 0.5 multiply_reduce_fusion
  15.7 0.0 copy-start.6
  15.7 0.0 copy-start.2
  15.7 0.6 fusion.68
  16.3 0.0 copy-done
  16.3 0.0 copy-done.10
  16.3 0.2 fusion.52
  16.5 0.0 copy-done.5
  16.5 0.1 fusion.26
  16.6 0.0 copy-done.9
  16.6 0.6 multiply_reduce_fusion.5
  17.2 41.5 %all-reduce = (f32[16]{0:T(128)S(1)}, f32[]{:T(128)}, f32[]{:T(128)}) all-reduce(f32[16]{0:T(128)S(1)} %fusion.26, f32[]{:T(128)} %fusion.68, f32[]{:T(128)} %multiply_reduce_fusion.5), channel_id=1, replica_groups=mesh['region'=4,'col'=8] {'region','col'}, use_global_device_ids=true, to_apply=%region_6.0 | all-reduce | flops 18 | bytes 144 | tf_op jit(solution)/shard_map/psum | solution.py:47
  60.2 0.0 reduce-scatter.3.cloned.1.call-done
  60.2 0.0 copy-done.3
  60.2 0.0 copy-done.8
  60.2 0.9 multiply_reduce_fusion.4
  61.1 12.9 %all_gather.6 = f32[16,16,128]{2,1,0:T(8,128)S(1)} all-gather(f32[2,16,128]{2,1,0:T(8,128)S(1)} %multiply_subtract_fusion.3), channel_id=1, replica_groups=mesh['region'=4,'col'=8] {'col'}, dimensions={0}, use_global_device_ids=true | all-gather | bytes 147456 | tf_op jit(solution)/shard_map/all_gather | solution.py:65
  74.0 0.4 fusion.23
  74.4 5.0 %fusion.16 = f32[48,16,128]{2,1,0:T(8,128)S(1)} fusion(f32[48,128,128]{2,1,0:T(8,128)S(1)} %copy-done.1, f32[48,16,128]{2,0,1:T(8,128)S(1)} %fusion.23), kind=kOutput, calls=%fused_computation.21 | convolution fusion | flops 150994944 | bytes 3932160 | tf_op jit(solution)/shard_map/tij,tsj->tsi/dot_general | solution.py:69
  79.4 0.0 copy-done.6
  79.4 0.4 fusion.6
  79.8 0.0 copy-done.2
  79.8 0.2 multiply_reduce_fusion.3
  80.0 13.3 %psum.67 = f32[16]{0:T(128)S(1)} all-reduce(f32[16]{0:T(128)S(1)} %get-tuple-element.26), channel_id=1, replica_groups=mesh['region'=4,'col'=8] {'col'}, use_global_device_ids=true, to_apply=%region_11.12 | all-reduce | flops 16 | bytes 128 | tf_op jit(solution)/shard_map/psum | solution.py:79
  93.3 42.8 %psum.66 = f32[16]{0:T(128)S(1)} all-reduce(f32[16]{0:T(128)S(1)} %get-tuple-element.24), channel_id=1, replica_groups=mesh['region'=4,'col'=8] {'region','col'}, use_global_device_ids=true, to_apply=%region_9.10 | all-reduce | flops 16 | bytes 128 | tf_op jit(solution)/shard_map/psum | solution.py:76
  136.1 8.2 %psum.68 = f32[16]{0:T(128)S(1)} all-reduce(f32[16]{0:T(128)S(1)} %psum.67), channel_id=1, replica_groups=mesh['region'=4,'col'=8] {'region'}, use_global_device_ids=true, to_apply=%region_12.13 | all-reduce | flops 16 | bytes 128 | tf_op jit(solution)/shard_map/psum | solution.py:80
  144.3 0.4 fusion.35
  144.7 2.9 %fusion.14 = f32[48,16,128]{2,1,0:T(8,128)S(1)} fusion(f32[48,128,128]{2,1,0:T(8,128)S(1)} %copy-done.1, f32[48,16,128]{2,0,1:T(8,128)S(1)} %fusion.35), kind=kOutput, calls=%fused_computation.19 | convolution fusion | flops 150994944 | bytes 3932160 | tf_op jit(solution)/shard_map/tij,tsi->tsj/dot_general | solution.py:57
  147.5 0.4 fusion.3
  148.0 0.7 copy.87
  148.7 0.0 reduce-scatter.5.cloned.1.call-update
  148.7 25.8 %reduce-scatter.5.cloned.1.call-done = f32[2,16,128]{2,1,0:T(8,128)} async-done(((f32[16,16,128]{2,1,0:T(8,128)}), f32[2,16,128]{2,1,0:T(8,128)}) %reduce-scatter.5.cloned.1.call-update) | async-done | bytes 16400 | tf_op jit(solution)/shard_map/reduce_scatter | solution.py:62
  174.6 0.9 multiply_reduce_fusion.2
  175.5 0.0 copy-start.4
  175.5 14.3 %all_gather.7 = f32[16,16,128]{2,1,0:T(8,128)S(1)} all-gather(f32[2,16,128]{2,1,0:T(8,128)S(1)} %multiply_subtract_fusion.2), channel_id=1, replica_groups=mesh['region'=4,'col'=8] {'col'}, dimensions={0}, use_global_device_ids=true | all-gather | bytes 147456 | tf_op jit(solution)/shard_map/all_gather | solution.py:65
  189.8 0.4 fusion.20
  190.1 5.0 %fusion.12 = f32[48,16,128]{2,1,0:T(8,128)S(1)} fusion(f32[48,128,128]{2,1,0:T(8,128)S(1)} %copy-done.1, f32[48,16,128]{2,0,1:T(8,128)S(1)} %fusion.20), kind=kOutput, calls=%fused_computation.17 | convolution fusion | flops 150994944 | bytes 3932160 | tf_op jit(solution)/shard_map/tij,tsj->tsi/dot_general | solution.py:69
  195.1 0.4 fusion
  195.6 0.8 multiply_reduce_fusion.1
  196.4 13.7 %psum.70 = f32[16]{0:T(128)S(1)} all-reduce(f32[16]{0:T(128)S(1)} %get-tuple-element.20), channel_id=1, replica_groups=mesh['region'=4,'col'=8] {'col'}, use_global_device_ids=true, to_apply=%region_17.18 | all-reduce | flops 16 | bytes 128 | tf_op jit(solution)/shard_map/psum | solution.py:79
  210.1 43.4 %psum.69 = f32[16]{0:T(128)S(1)} all-reduce(f32[16]{0:T(128)S(1)} %get-tuple-element.18), channel_id=1, replica_groups=mesh['region'=4,'col'=8] {'region','col'}, use_global_device_ids=true, to_apply=%region_15.16 | all-reduce | flops 16 | bytes 128 | tf_op jit(solution)/shard_map/psum | solution.py:76
  253.4 8.0 %psum.71 = f32[16]{0:T(128)S(1)} all-reduce(f32[16]{0:T(128)S(1)} %psum.70), channel_id=1, replica_groups=mesh['region'=4,'col'=8] {'region'}, use_global_device_ids=true, to_apply=%region_18.19 | all-reduce | flops 16 | bytes 128 | tf_op jit(solution)/shard_map/psum | solution.py:80
  261.4 0.5 multiply_sqrt_fusion
  262.0 0.0 copy-done.4
  (6 shorter events, 0.0 us)
Async XLA Ops:
  7.2 9.2 %copy-start = (f32[32,128]{1,0:T(8,128)S(1)}, f32[32,128]{1,0:T(8,128)}, u32[]{:S(2)}) copy-start(f32[32,128]{1,0:T(8,128)} %param.20) | copy-start | bytes 49156
  7.2 8.1 %copy-start.1 = (f32[48,128,128]{2,1,0:T(8,128)S(1)}, f32[48,128,128]{2,1,0:T(8,128)}, u32[]{:S(2)}) copy-start(f32[48,128,128]{2,1,0:T(8,128)} %param.11) | copy-start | bytes 9437188
  7.2 6.9 %copy-start.7 = (s32[48]{0:T(128)S(1)}, s32[48]{0:T(128)}, u32[]{:S(2)}) copy-start(s32[48]{0:T(128)} %param.13) | copy-start | bytes 580
  7.2 53.0 %reduce-scatter.3.cloned.1.call-start = ((), (), s32[]{:S(2)}) async-start(), calls=%async_computation.2 | async-start | bytes 147456 | tf_op jit(solution)/shard_map/reduce_scatter | solution.py:62
  9.3 7.0 %copy-start.10 = (s32[16]{0:T(128)S(1)}, s32[16]{0:T(128)}, u32[]{:S(2)}) copy-start(s32[16]{0:T(128)} %param.21) | copy-start | bytes 196
  9.3 7.2 %copy-start.5 = (f32[2,128]{1,0:T(2,128)S(1)}, f32[2,128]{1,0:T(2,128)}, u32[]{:S(2)}) copy-start(f32[2,128]{1,0:T(2,128)} %param.16) | copy-start | bytes 3076
  9.3 7.3 %copy-start.9 = (f32[2,128]{1,0:T(2,128)S(1)}, f32[2,128]{1,0:T(2,128)}, u32[]{:S(2)}) copy-start(f32[2,128]{1,0:T(2,128)} %param.15) | copy-start | bytes 3076
  9.3 50.9 %copy-start.3 = (f32[2,16,128]{2,1,0:T(8,128)S(1)}, f32[2,16,128]{2,1,0:T(8,128)}, u32[]{:S(2)}) copy-start(f32[2,16,128]{2,1,0:T(8,128)} %param.18) | copy-start | bytes 49156
  9.3 50.9 %copy-start.8 = (f32[2,128]{1,0:T(2,128)S(1)}, f32[2,128]{1,0:T(2,128)}, u32[]{:S(2)}) copy-start(f32[2,128]{1,0:T(2,128)} %param.17) | copy-start | bytes 3076
  15.2 159.4 %reduce-scatter.5.cloned.1.call-start = ((), (), s32[]{:S(2)}) async-start(), calls=%async_computation.3 | async-start | bytes 147456 | tf_op jit(solution)/shard_map/reduce_scatter | solution.py:62
  15.7 63.7 %copy-start.6 = (s32[48]{0:T(128)S(1)}, s32[48]{0:T(128)}, u32[]{:S(2)}) copy-start(s32[48]{0:T(128)} %param.12) | copy-start | bytes 580
  15.7 64.1 %copy-start.2 = (f32[2,16,128]{2,1,0:T(8,128)S(1)}, f32[2,16,128]{2,1,0:T(8,128)}, u32[]{:S(2)}) copy-start(f32[2,16,128]{2,1,0:T(8,128)} %param.19) | copy-start | bytes 49156
  175.5 86.5 %copy-start.4 = (f32[2,16,128]{2,1,0:T(8,128)}, f32[2,16,128]{2,1,0:T(8,128)S(1)}, u32[]{:S(2)}) copy-start(f32[2,16,128]{2,1,0:T(8,128)S(1)} %get-tuple-element.19) | copy-start | bytes 49156
Sparse Core Ops, SparseCore 0:
  15.3 27.7 reduce-scatter.2
  148.8 25.7 reduce-scatter.4
